TPU v7x, 512 devices: a whole 4x8x8 slice. The times are simulated.
512 devices in a mesh: kv: 16 (over z, core), ep: 32 (over x, y).
Axes of the slice: x: 4, y: 8, z: 8, core: 2. Of those that a mesh axis runs over, the one named last changes fastest.
Arguments:
- queries: bfloat16 [32, 64, 2048], P('ep'), may hold values from -12 to 12
- new_keys: bfloat16 [32, 64, 512], P('ep'), may hold values from -12 to 12
- new_values: bfloat16 [32, 64, 512], P('ep'), may hold values from -6 to 6
- cache_keys: bfloat16 [32, 64, 128, 512], P('ep', 'kv'), may hold values from -12 to 12
- cache_values: bfloat16 [32, 64, 128, 512], P('ep', 'kv'), may hold values from -10 to 10
- page_table: int32 [32, 64], P('ep'), may hold values from 0 to 63, each once within a row
- cached_len: int32 [32], P('ep'), may hold values from 1 to 8192, 65536 in all
- moe_rows: bfloat16 [1024, 4096], P('ep'), may hold values from -6 to 6
- expert_ids: int32 [1024, 2], P('ep'), may hold values from 0 to 7, all different within a row; in each aligned block of 32 rows (0 to 31, 32 to 63, ...) at most 16 rows name the same one
- gate_probs: float32 [1024, 2], P('ep'), may hold values from 0.1 to 0.9
- w_gate: bfloat16 [32, 4096, 2048], P('ep', None, 'kv'), may hold values from -0.09375 to 0.09375
- w_up: bfloat16 [32, 4096, 2048], P('ep', None, 'kv'), may hold values from -0.09375 to 0.09375
- w_down: bfloat16 [32, 2048, 4096], P('ep', 'kv'), may hold values from -0.09375 to 0.09375
Outputs:
- attn_out: bfloat16 [32, 64, 2048], P('ep')
- moe_out: bfloat16 [1024, 4096], P('ep', 'kv')
Inputs may be any that keep to these rules, and one draw needn't show every extreme that they name: `page_table`: each row is a permutation of the 64 slots of its request. `cached_len`: cached positions at or past a request's length hold no data. `expert_ids`: each row names 2 different experts; among the 32 rows of one ep index no expert is named more than 16 times, and this bound is reached.
All inputs are finite; a program needn't handle non-finite values. No bound on the sum of `cached_len` on one device may be relied on, other than what follows from the above.
Results may differ from a plain program's by a relative error of at most 0.0085.
Values may be sent and summed in bfloat16 or wider, within the bound.
No kernel may reach another device: no remote copies, remote signals or barrier semaphores. Data moves between devices by JAX's collectives and lax.ppermute only.
A program may use at most 128 MiB of HBM per device.

v0:
```python
import math
import jax
import jax.numpy as jnp
from jax import lax
from jax.sharding import PartitionSpec as P

HD = 128
EXPERTS = 8
TOP = 2
HQ = 16
KVH = 4
PAGE = 128
POOL_DEV = 4
CAP = 16
ROPE_BASE = 10000.0
MASKED = -1e30


def rotary(values, positions):
    half_width = values.shape[-1] // 2
    indices = jnp.arange(half_width, dtype=jnp.float32)
    frequency = jnp.power(ROPE_BASE, -2.0 * indices / values.shape[-1])
    angles = positions.astype(jnp.float32)[:, None] * frequency[None, :]
    cosine = jnp.cos(angles)[:, None, :]
    sine_part = jnp.sin(angles)[:, None, :]
    lower_half = values[..., :half_width]
    upper_half = values[..., half_width:]
    return jnp.concatenate(
        [
            lower_half * cosine - upper_half * sine_part,
            upper_half * cosine + lower_half * sine_part,
        ],
        axis=-1,
    )


def on_device(
    queries,
    new_keys,
    new_values,
    cache_keys,
    cache_values,
    page_table,
    cached_len,
    moe_rows,
    expert_ids,
    gate_probs,
    w_gate,
    w_up,
    w_down,
):
    kv_index = lax.axis_index("kv")
    kv_count = lax.axis_size("kv")
    all_rows = queries.shape[1]
    block_rows = all_rows // kv_count
    length = cached_len[0]
    group_size = HQ // KVH
    score_scale = 1.0 / math.sqrt(HD)
    slot_ids = kv_index * POOL_DEV + jnp.arange(POOL_DEV, dtype=jnp.int32)
    matches = (page_table[0][:, None] == slot_ids[None, :]).astype(jnp.int32)
    page_index = jnp.sum(
        matches * jnp.arange(page_table.shape[1], dtype=jnp.int32)[:, None], axis=0
    )
    cached_pos = (page_index[:, None] * PAGE + jnp.arange(PAGE, dtype=jnp.int32)[None, :]).reshape(
        -1
    )
    block_start = kv_index * block_rows
    own_pos = length + block_start + jnp.arange(block_rows, dtype=jnp.int32)
    key_block = lax.dynamic_slice_in_dim(new_keys[0], block_start, block_rows, 0)
    value_block = lax.dynamic_slice_in_dim(new_values[0], block_start, block_rows, 0)
    own_keys = rotary(key_block.astype(jnp.float32).reshape(block_rows, KVH, HD), own_pos).astype(
        jnp.bfloat16
    )
    local_keys = jnp.concatenate([cache_keys[0].reshape(-1, KVH, HD), own_keys], axis=0)
    local_values = jnp.concatenate(
        [cache_values[0].reshape(-1, KVH, HD), value_block.reshape(block_rows, KVH, HD)], axis=0
    )
    key_pos = jnp.concatenate([cached_pos, own_pos])
    live_keys = jnp.concatenate([cached_pos < length, jnp.ones((block_rows,), jnp.bool_)])
    positions = length + jnp.arange(all_rows, dtype=jnp.int32)
    rotated = rotary(queries[0].astype(jnp.float32).reshape(all_rows, HQ, HD), positions).astype(
        jnp.bfloat16
    )
    grouped = rotated.reshape(all_rows, KVH, group_size, HD)
    scores = (
        jnp.einsum("nkgd,mkd->nkgm", grouped, local_keys, preferred_element_type=jnp.float32)
        * score_scale
    )
    usable = (live_keys[None, :] & (key_pos[None, :] <= positions[:, None]))[:, None, None, :]
    scores = jnp.where(usable, scores, MASKED)
    part_high = jnp.max(scores, axis=-1)
    highest = lax.pmax(part_high, "kv")
    weights = jnp.where(usable, jnp.exp(scores - highest[..., None]), 0.0)
    part_total = jnp.sum(weights, axis=-1)
    part_blend = jnp.einsum(
        "nkgm,mkd->nkgd",
        weights.astype(jnp.bfloat16),
        local_values,
        preferred_element_type=jnp.float32,
    )
    total_row = jnp.pad(part_total.reshape(1, -1), ((0, 0), (0, HQ * HD - all_rows * HQ)))
    packed = lax.psum(
        jnp.concatenate([part_blend.reshape(all_rows, HQ * HD), total_row], axis=0), "kv"
    )
    row_total = packed[all_rows, : all_rows * HQ].reshape(all_rows, HQ)
    blended = packed[:all_rows].reshape(all_rows, HQ, HD)
    attn_out = (blended / row_total[..., None]).reshape(1, all_rows, HQ * HD).astype(jnp.bfloat16)
    ep_count = lax.axis_size("ep")
    share_count = ep_count // EXPERTS
    tok_rows = moe_rows.shape[0]
    slot_total = ep_count * CAP
    flat_ids = expert_ids.reshape(-1)
    one_hot = (flat_ids[:, None] == jnp.arange(EXPERTS, dtype=jnp.int32)[None, :]).astype(jnp.int32)
    earlier = jnp.cumsum(one_hot, axis=0) - one_hot
    slot_rank = jnp.sum(earlier * one_hot, axis=1)
    slot_index = jnp.arange(slot_total, dtype=jnp.int32)
    dest_expert = slot_index // CAP // share_count
    dest_slot = slot_index % CAP
    matched = (flat_ids[None, :] == dest_expert[:, None]) & (
        slot_rank[None, :] == dest_slot[:, None]
    )
    select = jnp.sum(matched.astype(jnp.float32).reshape(slot_total, tok_rows, TOP), axis=2).astype(
        jnp.bfloat16
    )
    weight_map = jnp.sum(
        jnp.where(matched, gate_probs.reshape(-1)[None, :], 0.0).reshape(slot_total, tok_rows, TOP),
        axis=2,
    )
    col_width = moe_rows.shape[1] // kv_count
    rows_cols = lax.dynamic_slice_in_dim(moe_rows, kv_index * col_width, col_width, 1)
    outgoing = (
        jnp.dot(select, rows_cols, preferred_element_type=jnp.float32)
        .astype(jnp.bfloat16)
        .reshape(ep_count, CAP, -1)
    )
    arrived_cols = lax.all_to_all(outgoing, "ep", split_axis=0, concat_axis=0, tiled=True).reshape(
        slot_total, -1
    )
    arrived = lax.all_gather(arrived_cols, "kv", axis=1, tiled=True)
    gate_proj = jnp.dot(arrived, w_gate[0], preferred_element_type=jnp.float32)
    up_proj = jnp.dot(arrived, w_up[0], preferred_element_type=jnp.float32)
    hidden = (jax.nn.silu(gate_proj) * up_proj).astype(jnp.bfloat16)
    out_width = w_down.shape[2] // kv_count
    down_split = w_down[0].reshape(w_down.shape[1], kv_count, out_width)
    down_cols = lax.all_to_all(down_split, "kv", split_axis=1, concat_axis=0, tiled=True).reshape(
        -1, out_width
    )
    summed = jnp.dot(
        lax.all_gather(hidden, "kv", axis=1, tiled=True),
        down_cols,
        preferred_element_type=jnp.float32,
    )
    returned = (
        lax.all_to_all(
            summed.reshape(ep_count, CAP, -1).astype(jnp.bfloat16),
            "ep",
            split_axis=0,
            concat_axis=0,
            tiled=True,
        )
        .astype(jnp.float32)
        .reshape(slot_total, -1)
    )
    moe_out = jnp.dot(
        weight_map.T, returned, precision=lax.Precision.HIGHEST, preferred_element_type=jnp.float32
    ).astype(jnp.bfloat16)
    return (attn_out, moe_out)


def solution(mesh):
    return jax.shard_map(
        on_device,
        mesh=mesh,
        in_specs=(
            P("ep", None, None),
            P("ep", None, None),
            P("ep", None, None),
            P("ep", "kv", None, None),
            P("ep", "kv", None, None),
            P("ep", None),
            P("ep"),
            P("ep", None),
            P("ep", None),
            P("ep", None),
            P("ep", None, "kv"),
            P("ep", None, "kv"),
            P("ep", "kv", None),
        ),
        out_specs=(P("ep", None, None), P("ep", "kv")),
        check_vma=False,
    )
```

profile of v0, /device:TPU:2, one launch (start us, length us, event | category | flops | bytes accessed | tf_op | source)
XLA Modules:
  0.0 277.6 jit_solution(767339811898479776)
XLA Ops:
  7.2 0.8 copy.46
  8.1 0.1 eq.71
  8.2 0.1 fusion.26
  8.3 0.1 reduce_window_sum.11
  8.4 0.2 select_reduce_fusion.1
  8.5 0.1 eq.75
  8.7 0.1 copy.47
  8.7 0.8 convert_reduce_fusion
  9.6 1.0 convolution_convert_fusion
  10.5 21.4 %all_to_all.25 = bf16[32,16,256]{2,1,0:T(8,128)(2,1)} all-to-all(bf16[32,16,256]{2,1,0:T(8,128)(2,1)S(1)} %bitcast.94), channel_id=1, replica_groups=mesh['kv'=16,'ep'=32] {'ep'}, dimensions={0} | all-to-all | bytes 524288 | tf_op jit(solution)/shard_map/all_to_all | solution.py:136
  32.0 1.5 copy.55
  33.5 1.3 copy.48
  34.8 10.5 %all-to-all-start.1 = ((bf16[128,16,256]{2,0,1:T(8,128)(2,1)}), bf16[128,16,256]{2,0,1:T(8,128)(2,1)S(1)}, u32[]{:S(2)}, u32[]{:S(2)}) async-start(bf16[128,16,256]{2,0,1:T(8,128)(2,1)} %copy.48), calls=%async_computation.1 | async-start | bytes 2097152 | tf_op jit(solution)/shard_map/all_to_all | solution.py:145
  46.1 0.1 copy.53
  46.2 1.2 reshape_squeeze.10
  47.4 0.9 copy.41
  48.3 0.2 select_reduce_fusion.2
  48.5 55.1 %all-gather.3.cloned.1.call-done = bf16[512,4096]{1,0:T(8,128)(2,1)} async-done(((bf16[512,256]{1,0:T(8,128)(2,1)}), bf16[512,4096]{1,0:T(8,128)(2,1)}) %all-gather.3.cloned.1.call-update) | async-done | bytes 4194320 | tf_op jit(solution)/shard_map/all_gather | solution.py:139
  103.5 3.6 %fusion.11 = f32[512,128]{1,0:T(8,128)S(1)} fusion(bf16[512,4096]{1,0:T(8,128)(2,1)} %all-gather.3.cloned.1.call-done, bf16[1,4096,128]{2,1,0:T(8,128)(2,1)S(1)} %copy-done), kind=kOutput, calls=%fused_computation.14 | convolution fusion | flops 536870912 | bytes 5505024 | tf_op jit(solution)/shard_map/dot_general | solution.py:140
  107.1 0.1 copy-done.5
  107.3 1.9 fusion.9
  109.3 0.1 broadcast_compare_fusion
  109.5 0.7 bitcast_convert_fusion
  110.2 0.1 multiply_cosine_fusion.1
  110.3 0.1 compare_and_fusion
  110.4 0.2 multiply_cosine_fusion
  110.6 0.1 subtract_convert_fusion.1
  110.7 0.2 fusion.48
  110.9 0.3 subtract_convert_fusion
  111.2 2.2 fusion
  113.5 24.3 %pmax.7 = f32[64,4,4]{0,2,1:T(4,128)S(1)} all-reduce(f32[64,4,4]{0,2,1:T(4,128)S(1)} %get-tuple-element.14), channel_id=1, replica_groups=mesh['kv'=16,'ep'=32] {'kv'}, use_global_device_ids=true, to_apply=%region_2.3 | all-reduce | flops 1024 | bytes 8192 | tf_op jit(solution)/shard_map/pmax | solution.py:92
  137.8 2.6 fusion.1
  140.4 0.1 copy.45
  140.5 0.2 reshape.299
  140.7 0.1 reshape_squeeze.9
  140.9 0.7 dynamic-slice_bitcast_fusion
  141.6 2.5 fusion.6
  144.1 0.3 copy.44
  144.5 0.2 reshape.298
  144.7 0.9 select_maximum_fusion
  145.6 3.0 %all-gather.5.cloned.1.call-done = bf16[512,2048]{1,0:T(8,128)(2,1)} async-done(((bf16[512,128]{1,0:T(8,128)(2,1)}), bf16[512,2048]{1,0:T(8,128)(2,1)}) %all-gather.5.cloned.1.call-update) | async-done | bytes 2097168 | tf_op jit(solution)/shard_map/all_gather | solution.py:149
  148.6 3.0 %convolution_convert_fusion.1 = bf16[32,16,256]{2,1,0:T(8,128)(2,1)} fusion(bf16[32,16,2048]{2,1,0:T(8,128)(2,1)} %bitcast.97, bf16[2048,256,1]{1,0,2:T(8,128)(2,1)S(1)} %bitcast.91), kind=kOutput, calls=%fused_computation.9 | convolution fusion | flops 537001984 | bytes 3407872 | tf_op jit(solution)/shard_map/dot_general | solution.py:148
  151.6 9.9 %all-to-all-start.2 = ((bf16[32,16,256]{2,1,0:T(8,128)(2,1)}), bf16[32,16,256]{2,1,0:T(8,128)(2,1)S(1)}, u32[]{:S(2)}, u32[]{:S(2)}) async-start(bf16[32,16,256]{2,1,0:T(8,128)(2,1)} %convolution_convert_fusion.1), calls=%async_computation.2 | async-start | bytes 524288 | tf_op jit(solution)/shard_map/all_to_all | solution.py:154
  161.5 105.7 %all-reduce.4.cloned.1.call-done = f32[65,2048]{1,0:T(8,128)} async-done(((f32[65,2048]{1,0:T(8,128)}), f32[65,2048]{1,0:T(8,128)}) %all-reduce.4.cloned.1.call-update) | async-done | bytes 532496 | tf_op jit(solution)/shard_map/psum | solution.py:102
  267.2 0.8 slice_reduce_fusion
  268.0 0.2 div.46
  268.2 1.9 fusion.24
  270.2 0.9 convolution_convert_fusion.2
  (33 shorter events, 0.5 us)
Async XLA Ops:
  7.2 96.4 %copy-start = (bf16[1,4096,128]{2,1,0:T(8,128)(2,1)S(1)}, bf16[1,4096,128]{2,1,0:T(8,128)(2,1)}, u32[]{:S(2)}) copy-start(bf16[1,4096,128]{2,1,0:T(8,128)(2,1)} %param.23) | copy-start | bytes 3145732
  7.2 96.3 %all-gather.3.cloned.1.call-start = ((), (), s32[]{:S(2)}) async-start(), calls=%async_computation.4 | async-start | bytes 4456448 | tf_op jit(solution)/shard_map/all_gather | solution.py:139
  33.5 12.6 %copy-start.4 = (bf16[1,64,2048]{2,1,0:T(8,128)(2,1)S(1)}, bf16[1,64,2048]{2,1,0:T(8,128)(2,1)}, u32[]{:S(2)}) copy-start(bf16[1,64,2048]{2,1,0:T(8,128)(2,1)} %param.13) | copy-start | bytes 786436
  34.8 13.5 %copy-start.6 = (s32[1,64]{1,0:T(1,128)S(1)}, s32[1,64]{1,0:T(1,128)}, u32[]{:S(2)}) copy-start(s32[1,64]{1,0:T(1,128)} %param.18) | copy-start | bytes 772
  34.8 110.8 %all-to-all-start.1 = ((bf16[128,16,256]{2,0,1:T(8,128)(2,1)}), bf16[128,16,256]{2,0,1:T(8,128)(2,1)S(1)}, u32[]{:S(2)}, u32[]{:S(2)}) async-start(bf16[128,16,256]{2,0,1:T(8,128)(2,1)} %copy.48), calls=%async_computation.1 | async-start | bytes 2097152 | tf_op jit(solution)/shard_map/all_to_all | solution.py:145
  45.4 103.2 %all-gather.5.cloned.1.call-start = ((), (), s32[]{:S(2)}) async-start(), calls=%async_computation.5 | async-start | bytes 2228224 | tf_op jit(solution)/shard_map/all_gather | solution.py:149
  103.5 3.6 %copy-start.1 = (bf16[512,4096]{1,0:T(8,128)(2,1)S(1)}, bf16[512,4096]{1,0:T(8,128)(2,1)}, u32[]{:S(2)}) copy-start(bf16[512,4096]{1,0:T(8,128)(2,1)} %all-gather.3.cloned.1.call-done) | copy-start | bytes 12582916
  103.5 3.7 %copy-start.5 = (bf16[1,4096,128]{2,1,0:T(8,128)(2,1)S(1)}, bf16[1,4096,128]{2,1,0:T(8,128)(2,1)}, u32[]{:S(2)}) copy-start(bf16[1,4096,128]{2,1,0:T(8,128)(2,1)} %param.24) | copy-start | bytes 3145732
  109.2 2.0 copy-start.3
  109.2 158.0 %all-reduce.4.cloned.1.call-start = ((), (), s32[]{:S(2)}) async-start(), calls=%async_computation.3 | async-start | bytes 1179648 | tf_op jit(solution)/shard_map/psum | solution.py:102
  111.2 29.5 %copy-start.2 = (bf16[1,4,128,512]{3,2,1,0:T(8,128)(2,1)S(1)}, bf16[1,4,128,512]{3,2,1,0:T(8,128)(2,1)}, u32[]{:S(2)}) copy-start(bf16[1,4,128,512]{3,2,1,0:T(8,128)(2,1)} %param.17) | copy-start | bytes 1572868
  151.6 118.6 %all-to-all-start.2 = ((bf16[32,16,256]{2,1,0:T(8,128)(2,1)}), bf16[32,16,256]{2,1,0:T(8,128)(2,1)S(1)}, u32[]{:S(2)}, u32[]{:S(2)}) async-start(bf16[32,16,256]{2,1,0:T(8,128)(2,1)} %convolution_convert_fusion.1), calls=%async_computation.2 | async-start | bytes 524288 | tf_op jit(solution)/shard_map/all_to_all | solution.py:154
Sparse Core Ops, SparseCore 0:
  32.1 71.3 all-gather.2
  109.3 39.2 all-gather.4
  150.9 116.2 all-reduce.3
where the time goes:
time: 278 us
  waiting for transfers between devices  164 us (59%)
  blocking collectives  45.7 us (16%)
  starting transfers between devices  20.6 us (7%)
  matrix products  15 us (5%)
  between operations  14.7 us (5%)
  local copies, waits for them, and re-layouts  9.25 us (3%)
  other arithmetic  8.53 us (3%)
    psum x1, waiting for transfers between devices, on_device(): lax.psum(jnp.concatenate([part_blend.reshape(all_rows, HQ * HD), total_ro...  106 us
    all_gather x1, waiting for transfers between devices, on_device(): arrived = lax.all_gather(arrived_cols, 'kv', axis=1, tiled=True)  55.1 us
    pmax x1, blocking collectives, on_device(): highest = lax.pmax(part_high, 'kv')  24.3 us
    all_to_all x1, blocking collectives, on_device(): lax.all_to_all(outgoing, 'ep', split_axis=0, concat_axis=0, tiled=True)  21.4 us
    all_to_all x1, starting transfers between devices, on_device(): lax.all_to_all(down_split, 'kv', split_axis=1, concat_axis=0, tiled=True)  10.5 us
    all_to_all x1, starting transfers between devices, on_device(): lax.all_to_all(summed.reshape(ep_count, CAP, -1).astype(jnp.bfloat16), 'e...  9.89 us
  transfers between devices with their start and end apart: 5, of which 3 were waited for; matrix products, arithmetic and copies ran while one was open for 10% of the time, Pallas kernels for 0%

commit v1 on v0

--- a/solution.py
+++ b/solution.py
@@ -14,6 +14,22 @@
 CAP = 16
 ROPE_BASE = 10000.0
 MASKED = -1e30
+
+
+def ring_gather(x, axis, dim):
+    ways, here, step = (lax.axis_size(axis), lax.axis_index(axis), x.shape[dim])
+    lengths = [n * ways if d == dim else n for d, n in enumerate(x.shape)]
+    full = lax.dynamic_update_slice_in_dim(jnp.zeros(lengths, x.dtype), x, here * step, axis=dim)
+    going_up = going_down = x
+    for far in range(1, ways // 2 + 1):
+        going_up = lax.ppermute(going_up, axis, [(d, (d + 1) % ways) for d in range(ways)])
+        full = lax.dynamic_update_slice_in_dim(full, going_up, (here - far) % ways * step, axis=dim)
+        if 2 * far < ways:
+            going_down = lax.ppermute(going_down, axis, [(d, (d - 1) % ways) for d in range(ways)])
+            full = lax.dynamic_update_slice_in_dim(
+                full, going_down, (here + far) % ways * step, axis=dim
+            )
+    return full
 
 
 def rotary(values, positions):
@@ -136,7 +152,7 @@
     arrived_cols = lax.all_to_all(outgoing, "ep", split_axis=0, concat_axis=0, tiled=True).reshape(
         slot_total, -1
     )
-    arrived = lax.all_gather(arrived_cols, "kv", axis=1, tiled=True)
+    arrived = ring_gather(arrived_cols, "kv", 1)
     gate_proj = jnp.dot(arrived, w_gate[0], preferred_element_type=jnp.float32)
     up_proj = jnp.dot(arrived, w_up[0], preferred_element_type=jnp.float32)
     hidden = (jax.nn.silu(gate_proj) * up_proj).astype(jnp.bfloat16)

time: 278 us -> 296 us (1.065)
  starting transfers between devices: 20.6 us -> 41.4 us
  waiting for transfers between devices: 164 us -> 154 us
  local copies, waits for them, and re-layouts: 9.25 us -> 16.1 us
    all_gather x1 -> x0, waiting for transfers between devices: 55.1 us -> none  [on_device(): arrived = lax.all_gather(arrived_cols, 'kv', axis=1, tiled=True)]
    ppermute x0 -> x15, waiting for transfers between devices: none -> 45.5 us  [the longest x7 27.6 us: ring_gather(): lax.ppermute(going_down, axis, [(d, (d - 1) % ways) for d in range(ways)])]
    ppermute x0 -> x15, starting transfers between devices: none -> 23.3 us  [the longest x7 23.3 us: ring_gather(): lax.ppermute(going_down, axis, [(d, (d - 1) % ways) for d in range(ways)])]
    dynamic_update_slice x0 -> x16, local copies, waits for them, and re-layouts: none -> 4.2 us  [the longest x8 2.1 us: ring_gather(): lax.dynamic_update_slice_in_dim(full, going_up, (here - far) % ways * ste...]
  transfers between devices with their start and end apart: 5 -> 19, of which waited for: 3 -> 12; matrix products, arithmetic and copies ran while one was open for 10% -> 12% of each run, Pallas kernels for 0% -> 0%
where the time goes in v1:
time: 296 us; the launch traced here: 295 us
  waiting for transfers between devices  154 us (52%)
  blocking collectives  45.7 us (15%)
  starting transfers between devices  41.4 us (14%)
  local copies, waits for them, and re-layouts  16.1 us (5%)
  between operations  15.4 us (5%)
  matrix products  13.9 us (5%)
  other arithmetic  8.53 us (3%)
    psum x1, waiting for transfers between devices, on_device(): lax.psum(jnp.concatenate([part_blend.reshape(all_rows, HQ * HD), total_ro...  105 us
    ppermute x7, waiting for transfers between devices, ring_gather(): lax.ppermute(going_down, axis, [(d, (d - 1) % ways) for d in range(ways)])  27.6 us
    pmax x1, blocking collectives, on_device(): highest = lax.pmax(part_high, 'kv')  24.4 us
    ppermute x7, starting transfers between devices, ring_gather(): lax.ppermute(going_down, axis, [(d, (d - 1) % ways) for d in range(ways)])  23.3 us
    all_to_all x1, blocking collectives, on_device(): lax.all_to_all(outgoing, 'ep', split_axis=0, concat_axis=0, tiled=True)  21.3 us
    ppermute x8, waiting for transfers between devices, ring_gather(): lax.ppermute(going_up, axis, [(d, (d + 1) % ways) for d in range(ways)])  18 us
    all_to_all x1, starting transfers between devices, on_device(): lax.all_to_all(summed.reshape(ep_count, CAP, -1).astype(jnp.bfloat16), 'e...  9.86 us
    all_to_all x1, starting transfers between devices, on_device(): lax.all_to_all(down_split, 'kv', split_axis=1, concat_axis=0, tiled=True)  8.11 us
  transfers between devices with their start and end apart: 19, of which 12 were waited for; matrix products, arithmetic and copies ran while one was open for 12% of the time, Pallas kernels for 0%

profile of v1, /device:TPU:2, one launch (start us, length us, event | category | flops | bytes accessed | tf_op | source)
XLA Modules:
  0.0 295.4 jit_solution(5883411364777420252)
XLA Ops:
  7.2 0.9 copy.46
  8.7 0.8 convert_reduce_fusion
  9.6 1.0 convolution_convert_fusion
  10.5 21.3 %all_to_all.25 = bf16[32,16,256]{2,1,0:T(8,128)(2,1)S(1)} all-to-all(bf16[32,16,256]{2,1,0:T(8,128)(2,1)S(1)} %bitcast.100), channel_id=1, replica_groups=mesh['kv'=16,'ep'=32] {'ep'}, dimensions={0} | all-to-all | bytes 524288 | tf_op jit(solution)/shard_map/all_to_all | solution.py:152
  31.8 5.4 %collective-permute-start.1 = (bf16[512,256]{1,0:T(8,128)(2,1)S(1)}, bf16[512,256]{1,0:T(8,128)(2,1)S(1)}, u32[]{:S(2)}, u32[]{:S(2)}) collective-permute-start(bf16[512,256]{1,0:T(8,128)(2,1)S(1)} %bitcast.95), channel_id=1, source_target_pairs={{0,480},{32,0},{64,32},{96,64},{128,96},{160,128},{192,160},{224,1... | collective-permute-start | bytes 786440 | tf_op jit(solution)/shard_map/ppermute | solution.py:28
  37.3 4.1 %collective-permute-done = bf16[512,256]{1,0:T(8,128)(2,1)S(1)} collective-permute-done((bf16[512,256]{1,0:T(8,128)(2,1)S(1)}, bf16[512,256]{1,0:T(8,128)(2,1)S(1)}, u32[]{:S(2)}, u32[]{:S(2)}) %collective-permute-start) | collective-permute-done | bytes 262176 | tf_op jit(solution)/shard_map/ppermute | solution.py:25
  41.3 1.6 copy.55
  42.9 1.3 copy.48
  44.2 8.1 %all-to-all-start.1 = ((bf16[128,16,256]{2,0,1:T(8,128)(2,1)}), bf16[128,16,256]{2,0,1:T(8,128)(2,1)S(1)}, u32[]{:S(2)}, u32[]{:S(2)}) async-start(bf16[128,16,256]{2,0,1:T(8,128)(2,1)} %copy.48), calls=%async_computation.1 | async-start | bytes 2097152 | tf_op jit(solution)/shard_map/all_to_all | solution.py:161
  52.4 2.9 collective-permute-start.3
  55.4 23.3 %collective-permute-done.3 = bf16[512,256]{1,0:T(8,128)(2,1)} collective-permute-done((bf16[512,256]{1,0:T(8,128)(2,1)S(1)}, bf16[512,256]{1,0:T(8,128)(2,1)}, u32[]{:S(2)}, u32[]{:S(2)}) %collective-permute-start.3) | collective-permute-done | bytes 262176 | tf_op jit(solution)/shard_map/ppermute | solution.py:28
  78.6 3.2 %collective-permute-start.5 = (bf16[512,256]{1,0:T(8,128)(2,1)}, bf16[512,256]{1,0:T(8,128)(2,1)}, u32[]{:S(2)}, u32[]{:S(2)}) collective-permute-start(bf16[512,256]{1,0:T(8,128)(2,1)} %collective-permute-done.3), channel_id=1, source_target_pairs={{0,480},{32,0},{64,32},{96,64},{128,96},{160,128},{192,160},{224,1... | collective-permute-start | bytes 786440 | tf_op jit(solution)/shard_map/ppermute | solution.py:28
  83.1 1.2 reshape_squeeze.10
  84.2 0.9 copy.41
  85.1 1.2 reshape_squeeze.9
  86.3 0.9 copy.40
  88.1 2.6 collective-permute-start.7
  90.8 3.6 %collective-permute-done.6 = bf16[512,256]{1,0:T(8,128)(2,1)S(1)} collective-permute-done((bf16[512,256]{1,0:T(8,128)(2,1)}, bf16[512,256]{1,0:T(8,128)(2,1)S(1)}, u32[]{:S(2)}, u32[]{:S(2)}) %collective-permute-start.6) | collective-permute-done | bytes 262176 | tf_op jit(solution)/shard_map/ppermute | solution.py:25
  94.4 1.0 constant_dynamic-update-slice_fusion.12
  95.4 1.0 constant_dynamic-update-slice_fusion.11
  96.4 3.0 %collective-permute-start.9 = (bf16[512,256]{1,0:T(8,128)(2,1)S(1)}, bf16[512,256]{1,0:T(8,128)(2,1)S(1)}, u32[]{:S(2)}, u32[]{:S(2)}) collective-permute-start(bf16[512,256]{1,0:T(8,128)(2,1)S(1)} %collective-permute-done.7), channel_id=1, source_target_pairs={{0,480},{32,0},{64,32},{96,64},{128,96},{160,128},{192,160},{224,1... | collective-permute-start | bytes 786440 | tf_op jit(solution)/shard_map/ppermute | solution.py:28
  99.3 1.0 constant_dynamic-update-slice_fusion.10
  100.3 1.1 collective-permute-done.8
  101.4 1.0 constant_dynamic-update-slice_fusion.9
  102.4 0.8 collective-permute-done.9
  103.2 3.1 %collective-permute-start.11 = (bf16[512,256]{1,0:T(8,128)(2,1)S(1)}, bf16[512,256]{1,0:T(8,128)(2,1)S(1)}, u32[]{:S(2)}, u32[]{:S(2)}) collective-permute-start(bf16[512,256]{1,0:T(8,128)(2,1)S(1)} %collective-permute-done.9), channel_id=1, source_target_pairs={{0,480},{32,0},{64,32},{96,64},{128,96},{160,128},{192,160},{224,1... | collective-permute-start | bytes 786440 | tf_op jit(solution)/shard_map/ppermute | solution.py:28
  106.4 2.0 collective-permute-done.10
  108.5 1.7 collective-permute-done.11
  110.2 3.1 %collective-permute-start.13 = (bf16[512,256]{1,0:T(8,128)(2,1)S(1)}, bf16[512,256]{1,0:T(8,128)(2,1)S(1)}, u32[]{:S(2)}, u32[]{:S(2)}) collective-permute-start(bf16[512,256]{1,0:T(8,128)(2,1)S(1)} %collective-permute-done.11), channel_id=1, source_target_pairs={{0,480},{32,0},{64,32},{96,64},{128,96},{160,128},{192,160},{224,1... | collective-permute-start | bytes 786440 | tf_op jit(solution)/shard_map/ppermute | solution.py:28
  113.4 2.0 collective-permute-done.12
  115.5 1.8 collective-permute-done.13
  117.3 5.2 %collective-permute-done.14 = bf16[512,256]{1,0:T(8,128)(2,1)S(1)} collective-permute-done((bf16[512,256]{1,0:T(8,128)(2,1)S(1)}, bf16[512,256]{1,0:T(8,128)(2,1)S(1)}, u32[]{:S(2)}, u32[]{:S(2)}) %collective-permute-start.14) | collective-permute-done | bytes 262176 | tf_op jit(solution)/shard_map/ppermute | solution.py:25
  122.5 1.2 fusion.11
  123.7 1.9 multiply_convert_fusion
  125.9 0.7 fusion.31
  127.7 3.2 %fusion = (f32[64,4,4]{0,2,1:T(4,128)S(1)}, f32[4,516,64,4]{1,2,3,0:T(8,128)}) fusion(pred[64,516]{1,0:T(8,128)(4,1)S(1)} %compare_and_fusion, bf16[64,4,4,64]{3,0,2,1:T(8,128)(2,1)S(1)} %bitcast.102, bf16[64,4,4,64]{3,0,2,1:T(8,128)(2,1)S(1)} %bitcast.101, bf16[4,4,64]{2,0,1:T(4,128)(2,1)S(1)} %get-tuple-element.9, ...), kind=kOutput, calls=%fused_computation.2 | convolution fusion | flops 138959872 | bytes 2941184 | tf_op jit(solution)/shard_map/nkgd,mkd->nkgm/dot_general | solution.py:102
  130.9 24.4 %pmax.7 = f32[64,4,4]{0,2,1:T(4,128)S(1)} all-reduce(f32[64,4,4]{0,2,1:T(4,128)S(1)} %get-tuple-element.14), channel_id=1, replica_groups=mesh['kv'=16,'ep'=32] {'kv'}, use_global_device_ids=true, to_apply=%region_2.3 | all-reduce | flops 1024 | bytes 8192 | tf_op jit(solution)/shard_map/pmax | solution.py:108
  155.3 0.7 fusion.29
  156.0 2.7 fusion.6
  159.2 2.6 fusion.1
  162.2 0.9 select_maximum_fusion
  163.1 3.3 %all-gather.2.cloned.1.call-done = bf16[512,2048]{1,0:T(8,128)(2,1)} async-done(((bf16[512,128]{1,0:T(8,128)(2,1)}), bf16[512,2048]{1,0:T(8,128)(2,1)}) %all-gather.2.cloned.1.call-update) | async-done | bytes 2097168 | tf_op jit(solution)/shard_map/all_gather | solution.py:165
  166.3 3.0 %convolution_convert_fusion.1 = bf16[32,16,256]{2,1,0:T(8,128)(2,1)} fusion(bf16[32,16,2048]{2,1,0:T(8,128)(2,1)} %bitcast.103, bf16[2048,256,1]{1,0,2:T(8,128)(2,1)S(1)} %bitcast.98), kind=kOutput, calls=%fused_computation.9 | convolution fusion | flops 537001984 | bytes 3407872 | tf_op jit(solution)/shard_map/dot_general | solution.py:164
  169.3 9.9 %all-to-all-start.2 = ((bf16[32,16,256]{2,1,0:T(8,128)(2,1)}), bf16[32,16,256]{2,1,0:T(8,128)(2,1)S(1)}, u32[]{:S(2)}, u32[]{:S(2)}) async-start(bf16[32,16,256]{2,1,0:T(8,128)(2,1)} %convolution_convert_fusion.1), calls=%async_computation.2 | async-start | bytes 524288 | tf_op jit(solution)/shard_map/all_to_all | solution.py:170
  179.2 105.5 %all-reduce.4.cloned.1.call-done = f32[65,2048]{1,0:T(8,128)} async-done(((f32[65,2048]{1,0:T(8,128)}), f32[65,2048]{1,0:T(8,128)}) %all-reduce.4.cloned.1.call-update) | async-done | bytes 532496 | tf_op jit(solution)/shard_map/psum | solution.py:118
  284.7 0.8 slice_reduce_fusion
  285.7 1.9 fusion.24
  287.7 0.9 convolution_convert_fusion.2
  (79 shorter events, 4.7 us)
Async XLA Ops:
  7.2 115.3 %copy-start = (bf16[1,4096,128]{2,1,0:T(8,128)(2,1)S(1)}, bf16[1,4096,128]{2,1,0:T(8,128)(2,1)}, u32[]{:S(2)}) copy-start(bf16[1,4096,128]{2,1,0:T(8,128)(2,1)} %param.23) | copy-start | bytes 3145732
  7.2 48.1 %copy-start.1 = (bf16[1,64,2048]{2,1,0:T(8,128)(2,1)S(1)}, bf16[1,64,2048]{2,1,0:T(8,128)(2,1)}, u32[]{:S(2)}) copy-start(bf16[1,64,2048]{2,1,0:T(8,128)(2,1)} %param.13) | copy-start | bytes 786436
  7.2 74.7 %copy-start.7 = (s32[1,64]{1,0:T(1,128)S(1)}, s32[1,64]{1,0:T(1,128)}, u32[]{:S(2)}) copy-start(s32[1,64]{1,0:T(1,128)} %param.18) | copy-start | bytes 772
  31.8 9.5 %collective-permute-start = (bf16[512,256]{1,0:T(8,128)(2,1)S(1)}, bf16[512,256]{1,0:T(8,128)(2,1)S(1)}, u32[]{:S(2)}, u32[]{:S(2)}) collective-permute-start(bf16[512,256]{1,0:T(8,128)(2,1)S(1)} %bitcast.94), channel_id=1, source_target_pairs={{0,32},{32,64},{64,96},{96,128},{128,160},{160,192},{192,224},{224... | collective-permute-start | bytes 786440 | tf_op jit(solution)/shard_map/ppermute | solution.py:25
  31.8 20.6 %collective-permute-start.1 = (bf16[512,256]{1,0:T(8,128)(2,1)S(1)}, bf16[512,256]{1,0:T(8,128)(2,1)S(1)}, u32[]{:S(2)}, u32[]{:S(2)}) collective-permute-start(bf16[512,256]{1,0:T(8,128)(2,1)S(1)} %bitcast.95), channel_id=1, source_target_pairs={{0,480},{32,0},{64,32},{96,64},{128,96},{160,128},{192,160},{224,1... | collective-permute-start | bytes 786440 | tf_op jit(solution)/shard_map/ppermute | solution.py:28
  41.3 14.0 %copy-start.4 = (bf16[512,256]{1,0:T(8,128)(2,1)}, bf16[512,256]{1,0:T(8,128)(2,1)S(1)}, u32[]{:S(2)}) copy-start(bf16[512,256]{1,0:T(8,128)(2,1)S(1)} %collective-permute-done) | copy-start | bytes 786436
  41.3 14.0 %collective-permute-start.2 = (bf16[512,256]{1,0:T(8,128)(2,1)S(1)}, bf16[512,256]{1,0:T(8,128)(2,1)}, u32[]{:S(2)}, u32[]{:S(2)}) collective-permute-start(bf16[512,256]{1,0:T(8,128)(2,1)S(1)} %collective-permute-done), channel_id=1, source_target_pairs={{0,32},{32,64},{64,96},{96,128},{128,160},{160,192},{192,224},{224... | collective-permute-start | bytes 786440 | tf_op jit(solution)/shard_map/ppermute | solution.py:25
  44.2 118.8 %all-to-all-start.1 = ((bf16[128,16,256]{2,0,1:T(8,128)(2,1)}), bf16[128,16,256]{2,0,1:T(8,128)(2,1)S(1)}, u32[]{:S(2)}, u32[]{:S(2)}) async-start(bf16[128,16,256]{2,0,1:T(8,128)(2,1)} %copy.48), calls=%async_computation.1 | async-start | bytes 2097152 | tf_op jit(solution)/shard_map/all_to_all | solution.py:161
  52.4 114.0 %all-gather.2.cloned.1.call-start = ((), (), s32[]{:S(2)}) async-start(), calls=%async_computation.4 | async-start | bytes 2228224 | tf_op jit(solution)/shard_map/all_gather | solution.py:165
  52.4 30.5 %copy-start.2 = (bf16[512,256]{1,0:T(8,128)(2,1)}, bf16[512,256]{1,0:T(8,128)(2,1)S(1)}, u32[]{:S(2)}) copy-start(bf16[512,256]{1,0:T(8,128)(2,1)S(1)} %collective-permute-done.1) | copy-start | bytes 786436
  52.4 26.2 %collective-permute-start.3 = (bf16[512,256]{1,0:T(8,128)(2,1)S(1)}, bf16[512,256]{1,0:T(8,128)(2,1)}, u32[]{:S(2)}, u32[]{:S(2)}) collective-permute-start(bf16[512,256]{1,0:T(8,128)(2,1)S(1)} %collective-permute-done.1), channel_id=1, source_target_pairs={{0,480},{32,0},{64,32},{96,64},{128,96},{160,128},{192,160},{224,1... | collective-permute-start | bytes 786440 | tf_op jit(solution)/shard_map/ppermute | solution.py:28
  55.3 31.8 %collective-permute-start.4 = (bf16[512,256]{1,0:T(8,128)(2,1)}, bf16[512,256]{1,0:T(8,128)(2,1)}, u32[]{:S(2)}, u32[]{:S(2)}) collective-permute-start(bf16[512,256]{1,0:T(8,128)(2,1)} %collective-permute-done.2), channel_id=1, source_target_pairs={{0,32},{32,64},{64,96},{96,128},{128,160},{160,192},{192,224},{224... | collective-permute-start | bytes 786440 | tf_op jit(solution)/shard_map/ppermute | solution.py:25
  78.6 9.5 %collective-permute-start.5 = (bf16[512,256]{1,0:T(8,128)(2,1)}, bf16[512,256]{1,0:T(8,128)(2,1)}, u32[]{:S(2)}, u32[]{:S(2)}) collective-permute-start(bf16[512,256]{1,0:T(8,128)(2,1)} %collective-permute-done.3), channel_id=1, source_target_pairs={{0,480},{32,0},{64,32},{96,64},{128,96},{160,128},{192,160},{224,1... | collective-permute-start | bytes 786440 | tf_op jit(solution)/shard_map/ppermute | solution.py:28
  87.1 0.9 copy-start.5
  87.2 3.6 %copy-start.3 = (bf16[512,256]{1,0:T(8,128)(2,1)S(1)}, bf16[512,256]{1,0:T(8,128)(2,1)}, u32[]{:S(2)}) copy-start(bf16[512,256]{1,0:T(8,128)(2,1)} %copy-done.2) | copy-start | bytes 786436
  87.2 7.2 %collective-permute-start.6 = (bf16[512,256]{1,0:T(8,128)(2,1)}, bf16[512,256]{1,0:T(8,128)(2,1)S(1)}, u32[]{:S(2)}, u32[]{:S(2)}) collective-permute-start(bf16[512,256]{1,0:T(8,128)(2,1)} %collective-permute-done.4), channel_id=1, source_target_pairs={{0,32},{32,64},{64,96},{96,128},{128,160},{160,192},{192,224},{224... | collective-permute-start | bytes 786440 | tf_op jit(solution)/shard_map/ppermute | solution.py:25
  88.1 8.2 %collective-permute-start.7 = (bf16[512,256]{1,0:T(8,128)(2,1)}, bf16[512,256]{1,0:T(8,128)(2,1)S(1)}, u32[]{:S(2)}, u32[]{:S(2)}) collective-permute-start(bf16[512,256]{1,0:T(8,128)(2,1)} %collective-permute-done.5), channel_id=1, source_target_pairs={{0,480},{32,0},{64,32},{96,64},{128,96},{160,128},{192,160},{224,1... | collective-permute-start | bytes 786440 | tf_op jit(solution)/shard_map/ppermute | solution.py:28
  94.4 7.0 %collective-permute-start.8 = (bf16[512,256]{1,0:T(8,128)(2,1)S(1)}, bf16[512,256]{1,0:T(8,128)(2,1)S(1)}, u32[]{:S(2)}, u32[]{:S(2)}) collective-permute-start(bf16[512,256]{1,0:T(8,128)(2,1)S(1)} %collective-permute-done.6), channel_id=1, source_target_pairs={{0,32},{32,64},{64,96},{96,128},{128,160},{160,192},{192,224},{224... | collective-permute-start | bytes 786440 | tf_op jit(solution)/shard_map/ppermute | solution.py:25
  96.4 6.9 %collective-permute-start.9 = (bf16[512,256]{1,0:T(8,128)(2,1)S(1)}, bf16[512,256]{1,0:T(8,128)(2,1)S(1)}, u32[]{:S(2)}, u32[]{:S(2)}) collective-permute-start(bf16[512,256]{1,0:T(8,128)(2,1)S(1)} %collective-permute-done.7), channel_id=1, source_target_pairs={{0,480},{32,0},{64,32},{96,64},{128,96},{160,128},{192,160},{224,1... | collective-permute-start | bytes 786440 | tf_op jit(solution)/shard_map/ppermute | solution.py:28
  101.4 7.0 %collective-permute-start.10 = (bf16[512,256]{1,0:T(8,128)(2,1)S(1)}, bf16[512,256]{1,0:T(8,128)(2,1)S(1)}, u32[]{:S(2)}, u32[]{:S(2)}) collective-permute-start(bf16[512,256]{1,0:T(8,128)(2,1)S(1)} %collective-permute-done.8), channel_id=1, source_target_pairs={{0,32},{32,64},{64,96},{96,128},{128,160},{160,192},{192,224},{224... | collective-permute-start | bytes 786440 | tf_op jit(solution)/shard_map/ppermute | solution.py:25
  103.2 7.0 %collective-permute-start.11 = (bf16[512,256]{1,0:T(8,128)(2,1)S(1)}, bf16[512,256]{1,0:T(8,128)(2,1)S(1)}, u32[]{:S(2)}, u32[]{:S(2)}) collective-permute-start(bf16[512,256]{1,0:T(8,128)(2,1)S(1)} %collective-permute-done.9), channel_id=1, source_target_pairs={{0,480},{32,0},{64,32},{96,64},{128,96},{160,128},{192,160},{224,1... | collective-permute-start | bytes 786440 | tf_op jit(solution)/shard_map/ppermute | solution.py:28
  108.4 7.0 %collective-permute-start.12 = (bf16[512,256]{1,0:T(8,128)(2,1)S(1)}, bf16[512,256]{1,0:T(8,128)(2,1)S(1)}, u32[]{:S(2)}, u32[]{:S(2)}) collective-permute-start(bf16[512,256]{1,0:T(8,128)(2,1)S(1)} %collective-permute-done.10), channel_id=1, source_target_pairs={{0,32},{32,64},{64,96},{96,128},{128,160},{160,192},{192,224},{224... | collective-permute-start | bytes 786440 | tf_op jit(solution)/shard_map/ppermute | solution.py:25
  108.5 15.2 %copy-start.6 = (bf16[1,4096,128]{2,1,0:T(8,128)(2,1)S(1)}, bf16[1,4096,128]{2,1,0:T(8,128)(2,1)}, u32[]{:S(2)}) copy-start(bf16[1,4096,128]{2,1,0:T(8,128)(2,1)} %param.24) | copy-start | bytes 3145732
  110.2 7.0 %collective-permute-start.13 = (bf16[512,256]{1,0:T(8,128)(2,1)S(1)}, bf16[512,256]{1,0:T(8,128)(2,1)S(1)}, u32[]{:S(2)}, u32[]{:S(2)}) collective-permute-start(bf16[512,256]{1,0:T(8,128)(2,1)S(1)} %collective-permute-done.11), channel_id=1, source_target_pairs={{0,480},{32,0},{64,32},{96,64},{128,96},{160,128},{192,160},{224,1... | collective-permute-start | bytes 786440 | tf_op jit(solution)/shard_map/ppermute | solution.py:28
  115.4 7.0 %collective-permute-start.14 = (bf16[512,256]{1,0:T(8,128)(2,1)S(1)}, bf16[512,256]{1,0:T(8,128)(2,1)S(1)}, u32[]{:S(2)}, u32[]{:S(2)}) collective-permute-start(bf16[512,256]{1,0:T(8,128)(2,1)S(1)} %collective-permute-done.12), channel_id=1, source_target_pairs={{0,32},{32,64},{64,96},{96,128},{128,160},{160,192},{192,224},{224... | collective-permute-start | bytes 786440 | tf_op jit(solution)/shard_map/ppermute | solution.py:25
  125.7 159.0 %all-reduce.4.cloned.1.call-start = ((), (), s32[]{:S(2)}) async-start(), calls=%async_computation.3 | async-start | bytes 1179648 | tf_op jit(solution)/shard_map/psum | solution.py:118
  169.3 118.4 %all-to-all-start.2 = ((bf16[32,16,256]{2,1,0:T(8,128)(2,1)}), bf16[32,16,256]{2,1,0:T(8,128)(2,1)S(1)}, u32[]{:S(2)}, u32[]{:S(2)}) async-start(bf16[32,16,256]{2,1,0:T(8,128)(2,1)} %convolution_convert_fusion.1), calls=%async_computation.2 | async-start | bytes 524288 | tf_op jit(solution)/shard_map/all_to_all | solution.py:170
Sparse Core Ops, SparseCore 0:
  125.8 40.4 all-gather.1
  168.7 115.9 all-reduce.3
